TPU v7x, 128 devices: a whole 4x4x4 slice. The times are simulated.
128 devices in a mesh: group: 8 (over y, core), member: 16 (over x, z).
Axes of the slice: x: 4, y: 4, z: 4, core: 2. Of those that a mesh axis runs over, the one named last changes fastest.
Arguments:
- queries: bfloat16 [2048, 64, 576], P(('group', 'member')), may hold values from -240 to 240
- latent_cache: bfloat16 [2048, 128, 576], P(('group', 'member')), may hold values from -4 to 4
- new_key: bfloat16 [2048, 576], P(('group', 'member')), may hold values from -4 to 4
- parent_beam: int32 [2048], P(('group', 'member')), may hold values from 0 to 3
- value_up: bfloat16 [64, 512, 128], P('member'), may hold values from -0.25 to 0.25
- out_proj: bfloat16 [8192, 3584], P('member', 'group'), may hold values from -0.0625 to 0.0625
- residual: bfloat16 [2048, 3584], P('member', 'group'), may hold values from -6 to 6
- expert_ids: int32 [2048, 8], P('member'), may hold values from 0 to 127, all different within a row; in each aligned block of 128 rows (0 to 127, 128 to 255, ...) at most 16 rows name the same one
- route_gates: float32 [2048, 8], P('member'), may hold values from 0.1 to 0.6
- w_gate: bfloat16 [128, 3584, 1024], P(('group', 'member')), may hold values from -0.09375 to 0.09375
- w_up: bfloat16 [128, 3584, 1024], P(('group', 'member')), may hold values from -0.09375 to 0.09375
- w_down: bfloat16 [128, 1024, 3584], P(('group', 'member')), may hold values from -0.1875 to 0.1875
Outputs:
- layer_out: bfloat16 [2048, 3584], P('member', 'group')
Inputs may be any that keep to these rules, and one draw needn't show every extreme that they name: `expert_ids`: each row names 8 different experts. Within each aligned block of 128 rows no expert is named by more than 16 rows, a bound that some block reaches.
All inputs are finite; a program needn't handle non-finite values.
Results may differ from a plain program's by a relative error of at most 0.019.
Values may be sent and summed in bfloat16 or wider, within the bound.
No kernel may reach another device: no remote copies, remote signals or barrier semaphores. Data moves between devices by JAX's collectives and lax.ppermute only.
A program may use at most 128 MiB of HBM per device.

v0:
```python
import jax
import jax.numpy as jnp
from jax import lax
from jax.sharding import PartitionSpec as P

ROPE = 64
VHEAD = 128
TOP = 8
BEAM = 4


def per_device(
    queries,
    latent_cache,
    new_key,
    parent_beam,
    value_up,
    out_proj,
    residual,
    expert_ids,
    route_gates,
    w_gate,
    w_up,
    w_down,
):
    rows = queries.shape[0]
    latent = value_up.shape[1]
    members = lax.axis_size("member")
    groups = lax.axis_size("group")
    experts = groups * members
    columns = out_proj.shape[1]
    scale = (VHEAD + ROPE) ** (-0.5)
    local_rows = jnp.arange(rows, dtype=jnp.int32)
    parent = local_rows // BEAM * BEAM + parent_beam
    keys = jnp.concatenate([jnp.take(latent_cache, parent, axis=0), new_key[:, None, :]], axis=1)
    chunks = 2
    step = rows // chunks
    pieces = []
    for c in range(chunks):
        asked = queries[c * step : (c + 1) * step]
        held = keys[c * step : (c + 1) * step]
        scores = jnp.einsum("rhw,rcw->rhc", asked, held, preferred_element_type=jnp.float32) * scale
        shifted = jnp.exp(scores - jnp.max(scores, axis=-1, keepdims=True))
        weights = (shifted / jnp.sum(shifted, axis=-1, keepdims=True)).astype(jnp.bfloat16)
        latent_out = jnp.einsum(
            "rhc,rcl->rhl", weights, held[:, :, :latent], preferred_element_type=jnp.float32
        ).astype(jnp.bfloat16)
        by_heads = lax.all_to_all(latent_out, "member", split_axis=1, concat_axis=0, tiled=True)
        per_head = jnp.einsum(
            "rhl,hlv->rhv", by_heads, value_up, preferred_element_type=jnp.float32
        ).astype(jnp.bfloat16)
        per_head = per_head.reshape(per_head.shape[0], per_head.shape[1] * per_head.shape[2])
        partial_sums = jnp.dot(
            lax.all_gather(per_head, "group", axis=0, tiled=True),
            out_proj,
            preferred_element_type=jnp.float32,
        )
        arrived_sums = lax.all_to_all(
            partial_sums.astype(jnp.bfloat16).reshape(members, -1, columns),
            "member",
            split_axis=0,
            concat_axis=0,
            tiled=True,
        )
        summed = jnp.sum(arrived_sums.astype(jnp.float32), axis=0)
        pieces.append(summed.reshape(-1, step, columns))
    attention = jnp.stack(pieces, axis=1).reshape(-1, columns)
    hidden_in = (residual.astype(jnp.float32) + attention).astype(jnp.bfloat16)
    block_rows = hidden_in.shape[0]
    capacity = max(2, 2 * rows * TOP // members)
    flat_ids = expert_ids.reshape(-1)
    onehot = (flat_ids[:, None] == jnp.arange(experts, dtype=jnp.int32)[None, :]).astype(jnp.int32)
    ranking = jnp.sum((jnp.cumsum(onehot, axis=0) - onehot) * onehot, axis=1)
    slot_index = flat_ids * capacity + ranking
    positions = jnp.arange(experts * capacity, dtype=jnp.int32)
    matches = (positions[:, None] == slot_index[None, :]).reshape(
        experts * capacity, block_rows, TOP
    )
    send_map = jnp.any(matches, axis=2).astype(jnp.bfloat16)
    outgoing = jnp.dot(send_map, hidden_in, preferred_element_type=jnp.float32).astype(jnp.bfloat16)
    arrived = lax.all_to_all(
        outgoing.reshape(experts, capacity, columns),
        ("group", "member"),
        split_axis=0,
        concat_axis=0,
        tiled=True,
    )
    expert_rows = (
        arrived.reshape(groups, members, capacity, columns)
        .transpose(1, 2, 0, 3)
        .reshape(members * capacity, groups * columns)
    )
    gate = jnp.dot(expert_rows, w_gate[0], preferred_element_type=jnp.float32)
    upper = jnp.dot(expert_rows, w_up[0], preferred_element_type=jnp.float32)
    inner = (jax.nn.silu(gate) * upper).astype(jnp.bfloat16)
    results = jnp.dot(inner, w_down[0], preferred_element_type=jnp.float32).astype(jnp.bfloat16)
    arranged = (
        results.reshape(members, capacity, groups, columns)
        .transpose(2, 0, 1, 3)
        .reshape(experts, capacity, columns)
    )
    returned = lax.all_to_all(
        arranged, ("group", "member"), split_axis=0, concat_axis=0, tiled=True
    )
    returned = returned.reshape(experts * capacity, columns)
    picked = returned[slot_index.reshape(block_rows, TOP)].astype(jnp.float32)
    mixed = jnp.sum(route_gates[:, :, None] * picked, axis=1)
    return (hidden_in.astype(jnp.float32) + mixed).astype(jnp.bfloat16)


def solution(mesh):
    in_specs = (
        P(("group", "member"), None, None),
        P(("group", "member"), None, None),
        P(("group", "member"), None),
        P(("group", "member")),
        P("member", None, None),
        P("member", "group"),
        P("member", "group"),
        P("member", None),
        P("member", None),
        P(("group", "member"), None, None),
        P(("group", "member"), None, None),
        P(("group", "member"), None, None),
    )
    out_specs = P("member", "group")
    return jax.shard_map(
        per_device, mesh=mesh, in_specs=in_specs, out_specs=out_specs, check_vma=False
    )
```

profile of v0, /device:TPU:1, one launch (start us, length us, event | category | flops | bytes accessed | tf_op | source)
XLA Modules:
  0.0 237.2 jit_solution(4019409785269201127)
XLA Ops:
  6.5 0.8 compare_and_fusion
  7.4 0.9 copy-done
  8.2 2.3 gather_fusion
  10.5 4.3 %copy.88 = bf16[16,128,576]{2,1,0:T(8,128)(2,1)} copy(bf16[16,128,576]{1,2,0:T(8,128)(2,1)} %gather_fusion) | data formatting | bytes 4718592 | tf_op jit(solution)/shard_map/jit(_take)/gather | solution.py:35
  14.9 0.0 copy-start.9
  14.9 2.2 broadcast_select_fusion
  17.1 0.7 fusion.26
  17.8 0.8 copy-done.2
  18.6 0.2 fusion.62
  18.8 0.0 copy-start.3
  18.8 2.3 convolution_convert_fusion.4
  21.2 0.3 copy.90
  21.5 18.6 %all_to_all.56 = bf16[8,64,512]{2,0,1:T(8,128)(2,1)S(1)} all-to-all(bf16[8,64,512]{2,0,1:T(8,128)(2,1)S(1)} %copy.90), channel_id=1, replica_groups=mesh['group'=8,'member'=16] {'member'}, dimensions={1} | all-to-all | bytes 1048576 | tf_op jit(solution)/shard_map/all_to_all | solution.py:48
  40.1 1.0 convolution_convert_fusion.6
  41.0 0.0 all-gather.3.cloned.1.call-update
  41.1 0.0 all-gather.5.cloned.1.call-start
  41.1 2.2 fusion.28
  43.3 0.2 fusion.61
  43.5 2.3 convolution_convert_fusion.3
  45.8 0.3 copy.94
  46.1 12.5 %all_to_all.57 = bf16[8,64,512]{2,0,1:T(8,128)(2,1)S(1)} all-to-all(bf16[8,64,512]{2,0,1:T(8,128)(2,1)S(1)} %copy.94), channel_id=1, replica_groups=mesh['group'=8,'member'=16] {'member'}, dimensions={1} | all-to-all | bytes 1048576 | tf_op jit(solution)/shard_map/all_to_all | solution.py:48
  58.6 1.0 convolution_convert_fusion.5
  59.6 0.0 all-gather.5.cloned.1.call-update
  59.6 4.7 %all-gather.3.cloned.1.call-done = bf16[1024,512]{0,1:T(8,128)(2,1)} async-done(((bf16[128,512]{0,1:T(8,128)(2,1)}), bf16[1024,512]{0,1:T(8,128)(2,1)}) %all-gather.3.cloned.1.call-update) | async-done | bytes 1048592 | tf_op jit(solution)/shard_map/all_gather | solution.py:54
  64.3 1.9 convolution_convert_fusion.2
  66.2 0.0 copy-start.7
  66.2 1.3 copy.93
  67.5 6.7 %all-to-all-start.1 = ((bf16[16,64,448]{2,1,0:T(8,128)(2,1)}), bf16[16,64,448]{2,1,0:T(8,128)(2,1)S(1)}, u32[]{:S(2)}, u32[]{:S(2)}) async-start(bf16[16,64,448]{2,1,0:T(8,128)(2,1)} %bitcast.7), calls=%async_computation.1 | async-start | bytes 2097152 | tf_op jit(solution)/shard_map/all_to_all | solution.py:58
  74.2 0.1 copy.100
  74.3 0.1 eq.44
  74.4 0.1 copy.102
  74.5 0.2 fusion.46
  74.8 15.5 %all-gather.5.cloned.1.call-done = bf16[1024,512]{0,1:T(8,128)(2,1)} async-done(((bf16[128,512]{0,1:T(8,128)(2,1)}), bf16[1024,512]{0,1:T(8,128)(2,1)}) %all-gather.5.cloned.1.call-update) | async-done | bytes 1048592 | tf_op jit(solution)/shard_map/all_gather | solution.py:54
  90.2 1.9 convolution_convert_fusion.1
  92.1 0.0 copy-start.5
  92.1 1.3 copy.97
  93.4 0.0 all-to-all-done.1
  93.4 6.7 %all-to-all-start.3 = ((bf16[16,64,448]{2,1,0:T(8,128)(2,1)}), bf16[16,64,448]{2,1,0:T(8,128)(2,1)S(1)}, u32[]{:S(2)}, u32[]{:S(2)}) async-start(bf16[16,64,448]{2,1,0:T(8,128)(2,1)} %bitcast.15), calls=%async_computation.3 | async-start | bytes 2097152 | tf_op jit(solution)/shard_map/all_to_all | solution.py:58
  100.2 0.1 eq.40
  100.3 0.1 copy.87
  100.4 0.1 copy.103
  100.5 0.4 fusion.40
  100.9 0.1 reduce_sum.61
  101.0 7.4 %fusion.2 = pred[2048,128]{1,0:T(8,128)(4,1)S(1)} fusion(s32[128,8]{0,1:T(8,128)S(1)} %get-tuple-element.6), kind=kLoop, calls=%fused_computation.5 | loop fusion | flops 3932160 | bytes 266240 | tf_op jit(solution)/shard_map/reduce_or | solution.py:79
  108.5 0.2 convert_reduce_fusion.1
  108.6 7.3 %all-to-all-done.3 = bf16[16,64,448]{2,1,0:T(8,128)(2,1)S(1)} async-done(((bf16[16,64,448]{2,1,0:T(8,128)(2,1)}), bf16[16,64,448]{2,1,0:T(8,128)(2,1)S(1)}, u32[]{:S(2)}, u32[]{:S(2)}) %all-to-all-start.3) | async-done | bytes 917536 | tf_op jit(solution)/shard_map/all_to_all | solution.py:58
  115.9 0.2 convert_reduce_fusion
  116.2 1.9 convolution_convert_fusion
  118.1 2.8 %copy.105 = bf16[2048,448]{1,0:T(8,128)(2,1)S(1)} copy(bf16[2048,448]{0,1:T(8,128)(2,1)} %convolution_convert_fusion) | data formatting | bytes 3670016 | tf_op jit(solution)/shard_map/convert_element_type | solution.py:80
  120.9 37.5 %all_to_all.58 = bf16[128,16,448]{2,1,0:T(8,128)(2,1)S(1)} all-to-all(bf16[128,16,448]{2,1,0:T(8,128)(2,1)S(1)} %bitcast.86), channel_id=1, replica_groups=mesh['group'=8,'member'=16] {'group','member'}, dimensions={0} | all-to-all | bytes 3670016 | tf_op jit(solution)/shard_map/all_to_all | solution.py:81
  158.5 1.4 copy.121
  159.9 3.3 %reshape.88 = bf16[256,3584]{1,0:T(8,128)(2,1)} reshape(bf16[16,16,8,448]{3,2,1,0:T(8,128)(2,1)S(1)} %bitcast.88) | data formatting | bytes 3670016 | tf_op jit(solution)/shard_map/reshape | solution.py:91
  163.2 6.8 %fusion.7 = f32[256,1024]{1,0:T(8,128)} fusion(bf16[256,3584]{1,0:T(8,128)(2,1)} %reshape.88, bf16[1,3584,1024]{2,1,0:T(8,128)(2,1)} %param.21), kind=kOutput, calls=%fused_computation.10 | convolution fusion | flops 1879048192 | bytes 10223616 | tf_op jit(solution)/shard_map/dot_general | solution.py:93
  170.0 10.8 %fusion.9 = bf16[256,3584]{1,0:T(8,128)(2,1)} fusion(bf16[1,1024,3584]{2,1,0:T(8,128)(2,1)} %param.23, bf16[256,3584]{1,0:T(8,128)(2,1)S(1)} %copy-done.4, bf16[1,3584,1024]{2,1,0:T(8,128)(2,1)} %param.22, f32[256,1024]{1,0:T(8,128)} %fusion.7), kind=kOutput, calls=%fused_computation.12 | convolution fusion | flops 3760586752 | bytes 19398656 | tf_op jit(solution)/shard_map/dot_general | solution.py:96
  180.8 3.9 %reshape.89 = bf16[16,16,8,448]{3,2,1,0:T(8,128)(2,1)S(1)} reshape(bf16[256,3584]{1,0:T(8,128)(2,1)} %fusion.9) | data formatting | bytes 3670016 | tf_op jit(solution)/shard_map/reshape | solution.py:98
  184.7 2.0 copy.107
  186.7 5.8 %all-to-all-start.5 = ((bf16[128,16,448]{2,1,0:T(8,128)(2,1)}), bf16[128,16,448]{2,1,0:T(8,128)(2,1)}, u32[]{:S(2)}, u32[]{:S(2)}) async-start(bf16[128,16,448]{2,1,0:T(8,128)(2,1)} %bitcast.28), calls=%async_computation.5 | async-start | bytes 4194304 | tf_op jit(solution)/shard_map/all_to_all | solution.py:102
  192.6 0.1 copy.108
  192.7 0.1 reshape.102
  192.8 0.7 copy.99
  193.5 28.5 %all-to-all-done.5 = bf16[128,16,448]{2,1,0:T(8,128)(2,1)} async-done(((bf16[128,16,448]{2,1,0:T(8,128)(2,1)}), bf16[128,16,448]{2,1,0:T(8,128)(2,1)}, u32[]{:S(2)}, u32[]{:S(2)}) %all-to-all-start.5) | async-done | bytes 1835040 | tf_op jit(solution)/shard_map/all_to_all | solution.py:102
  222.0 6.0 %gather_fusion.1 = bf16[1024,448]{1,0:T(8,128)(2,1)S(1)} fusion(bf16[2048,448]{1,0:T(8,128)(2,1)} %bitcast.29, s32[1024]{0:T(1024)S(1)} %broadcast_clamp_fusion), kind=kCustom, calls=%fused_computation.1 | custom fusion | bytes 1839104 | tf_op jit(solution)/shard_map/gather | solution.py:106
  228.0 1.6 fusion.12
  229.6 0.8 copy.109
  (30 shorter events, 0.3 us)
Async XLA Ops:
  6.5 1.7 copy-start
  6.5 57.8 %all-gather.3.cloned.1.call-start = ((), (), s32[]{:S(2)}) async-start(), calls=%async_computation.6 | async-start | bytes 1179648 | tf_op jit(solution)/shard_map/all_gather | solution.py:54
  10.5 4.3 %copy-start.6 = (bf16[16,576]{1,0:T(8,128)(2,1)S(1)}, bf16[16,576]{1,0:T(8,128)(2,1)}, u32[]{:S(2)}) copy-start(bf16[16,576]{1,0:T(8,128)(2,1)} %param.14) | copy-start | bytes 55300
  14.9 2.2 copy-start.9
  17.1 1.5 copy-start.2
  18.8 21.2 %copy-start.3 = (bf16[4,512,128]{2,1,0:T(8,128)(2,1)S(1)}, bf16[4,512,128]{2,1,0:T(8,128)(2,1)}, u32[]{:S(2)}) copy-start(bf16[4,512,128]{2,1,0:T(8,128)(2,1)} %param.16) | copy-start | bytes 1572868
  41.1 49.2 %all-gather.5.cloned.1.call-start = ((), (), s32[]{:S(2)}) async-start(), calls=%async_computation.7 | async-start | bytes 1179648 | tf_op jit(solution)/shard_map/all_gather | solution.py:54
  45.8 18.5 %copy-start.10 = (bf16[512,448]{0,1:T(8,128)(2,1)S(1)}, bf16[512,448]{0,1:T(8,128)(2,1)}, u32[]{:S(2)}) copy-start(bf16[512,448]{0,1:T(8,128)(2,1)} %param.17) | copy-start | bytes 1376260
  66.2 8.0 %copy-start.7 = (s32[128,8]{0,1:T(8,128)S(1)}, s32[128,8]{0,1:T(8,128)}, u32[]{:S(2)}) copy-start(s32[128,8]{0,1:T(8,128)} %param.19) | copy-start | bytes 12292
  67.5 25.9 %all-to-all-start.1 = ((bf16[16,64,448]{2,1,0:T(8,128)(2,1)}), bf16[16,64,448]{2,1,0:T(8,128)(2,1)S(1)}, u32[]{:S(2)}, u32[]{:S(2)}) async-start(bf16[16,64,448]{2,1,0:T(8,128)(2,1)} %bitcast.7), calls=%async_computation.1 | async-start | bytes 2097152 | tf_op jit(solution)/shard_map/all_to_all | solution.py:58
  92.1 8.2 %copy-start.5 = (bf16[128,448]{0,1:T(8,128)(2,1)S(1)}, bf16[128,448]{0,1:T(8,128)(2,1)}, u32[]{:S(2)}) copy-start(bf16[128,448]{0,1:T(8,128)(2,1)} %param.18) | copy-start | bytes 344068
  93.4 22.5 %all-to-all-start.3 = ((bf16[16,64,448]{2,1,0:T(8,128)(2,1)}), bf16[16,64,448]{2,1,0:T(8,128)(2,1)S(1)}, u32[]{:S(2)}, u32[]{:S(2)}) async-start(bf16[16,64,448]{2,1,0:T(8,128)(2,1)} %bitcast.15), calls=%async_computation.3 | async-start | bytes 2097152 | tf_op jit(solution)/shard_map/all_to_all | solution.py:58
  163.2 6.8 %copy-start.4 = (bf16[256,3584]{1,0:T(8,128)(2,1)S(1)}, bf16[256,3584]{1,0:T(8,128)(2,1)}, u32[]{:S(2)}) copy-start(bf16[256,3584]{1,0:T(8,128)(2,1)} %reshape.88) | copy-start | bytes 5505028
  186.7 6.1 %copy-start.8 = (f32[128,8]{0,1:T(8,128)S(1)}, f32[128,8]{0,1:T(8,128)}, u32[]{:S(2)}) copy-start(f32[128,8]{0,1:T(8,128)} %param.20) | copy-start | bytes 12292
  186.7 35.3 %all-to-all-start.5 = ((bf16[128,16,448]{2,1,0:T(8,128)(2,1)}), bf16[128,16,448]{2,1,0:T(8,128)(2,1)}, u32[]{:S(2)}, u32[]{:S(2)}) async-start(bf16[128,16,448]{2,1,0:T(8,128)(2,1)} %bitcast.28), calls=%async_computation.5 | async-start | bytes 4194304 | tf_op jit(solution)/shard_map/all_to_all | solution.py:102
  222.0 8.4 %copy-start.1 = (bf16[16,128,576]{1,2,0:T(8,128)(2,1)S(1)}, bf16[16,128,576]{1,2,0:T(8,128)(2,1)}, u32[]{:S(2)}) copy-start(bf16[16,128,576]{1,2,0:T(8,128)(2,1)} %param.13) | copy-start | bytes 7077892
Sparse Core Ops, SparseCore 0:
  41.2 23.0 all-gather.2
  66.0 24.2 all-gather.4
where the time goes:
time: 238 us; the launch traced here: 237 us
  blocking collectives  68.6 us (29%)
  waiting for transfers between devices  55.9 us (23%)
  local copies, waits for them, and re-layouts  33.5 us (14%)
  matrix products  32.7 us (14%)
  starting transfers between devices  19.2 us (8%)
  between operations  13.7 us (6%)
  other arithmetic  13.5 us (6%)
    all_to_all x1, blocking collectives, per_device(): lax.all_to_all(outgoing.reshape(experts, capacity, columns), ('group', 'm...  37.5 us
    all_to_all x2, blocking collectives, per_device(): lax.all_to_all(latent_out, 'member', split_axis=1, concat_axis=0, tiled=T...  31.1 us
    all_to_all x1, waiting for transfers between devices, per_device(): lax.all_to_all(arranged, ('group', 'member'), split_axis=0, concat_axis=0...  28.5 us
    all_gather x2, waiting for transfers between devices, per_device(): lax.all_gather(per_head, 'group', axis=0, tiled=True)  20.2 us
    all_to_all x2, starting transfers between devices, per_device(): lax.all_to_all(partial_sums.astype(jnp.bfloat16).reshape(members, -1, col...  13.4 us
    dot_general x1, matrix products, per_device(): jnp.dot(inner, w_down[0], preferred_element_type=jnp.float32)  10.8 us
    reduce_or x1, other arithmetic, per_device(): send_map = jnp.any(matches, axis=2).astype(jnp.bfloat16)  7.43 us
    all_to_all x2, waiting for transfers between devices, per_device(): lax.all_to_all(partial_sums.astype(jnp.bfloat16).reshape(members, -1, col...  7.28 us
  transfers between devices with their start and end apart: 5, of which 4 were waited for; matrix products, arithmetic and copies ran while one was open for 9% of the time, Pallas kernels for 0%

commit v1 on v0

--- a/solution.py
+++ b/solution.py
@@ -2,11 +2,46 @@
 import jax.numpy as jnp
 from jax import lax
 from jax.sharding import PartitionSpec as P
+from jax.lax import axis_index, ppermute, psum
 
 ROPE = 64
 VHEAD = 128
 TOP = 8
 BEAM = 4
+
+
+def levels_all_put(v0):
+    front, piece_next, local_next = (psum(1, "group"), axis_index("group"), v0.shape[0])
+    xs_all = []
+    for ii, num in enumerate(v0.shape):
+        xs_all.append(num * front if ii == 0 else num)
+    extra = new = v0
+    back = lax.dynamic_update_slice_in_dim(
+        jnp.zeros(xs_all, v0.dtype), v0, piece_next * local_next, axis=0
+    )
+    no = 1
+    while no < front // 2 + 1:
+        tray = []
+        ii = 0
+        while ii < front:
+            tray.append((ii, (ii + 1) % front))
+            ii = ii + 1
+        extra = ppermute(extra, "group", tray)
+        back = lax.dynamic_update_slice_in_dim(
+            back, extra, (piece_next - no) % front * local_next, axis=0
+        )
+        if 2 * no < front:
+            crops = []
+            ii = 0
+            while ii < front:
+                crops.append((ii, (ii - 1) % front))
+                ii += 1
+            new = ppermute(new, "group", crops)
+            back = lax.dynamic_update_slice_in_dim(
+                back, new, (piece_next + no) % front * local_next, axis=0
+            )
+        no = no + 1
+    return back
 
 
 def per_device(
@@ -51,9 +86,7 @@
         ).astype(jnp.bfloat16)
         per_head = per_head.reshape(per_head.shape[0], per_head.shape[1] * per_head.shape[2])
         partial_sums = jnp.dot(
-            lax.all_gather(per_head, "group", axis=0, tiled=True),
-            out_proj,
-            preferred_element_type=jnp.float32,
+            levels_all_put(per_head), out_proj, preferred_element_type=jnp.float32
         )
         arrived_sums = lax.all_to_all(
             partial_sums.astype(jnp.bfloat16).reshape(members, -1, columns),

time: 238 us -> 228 us (0.958)
  starting transfers between devices: 19.2 us -> 44.4 us
  blocking collectives: 68.6 us -> 47 us
  between operations: 13.7 us -> 0.66 us
  local copies, waits for them, and re-layouts: 33.5 us -> 36.9 us
  matrix products: 32.7 us -> 30 us
    all_to_all x2 -> x0, blocking collectives: 31.1 us -> none  [per_device(): lax.all_to_all(latent_out, 'member', split_axis=1, concat_axis=0, tiled=T...]
    all_gather x2 -> x0, waiting for transfers between devices: 20.2 us -> none  [per_device(): lax.all_gather(per_head, 'group', axis=0, tiled=True)]
    ppermute x0 -> x14, starting transfers between devices: none -> 18.9 us  [the longest x8 14.4 us: levels_all_put(): extra = ppermute(extra, 'group', tray)]
    all_to_all x0 -> x2, starting transfers between devices: none -> 12 us  [per_device(): lax.all_to_all(latent_out, 'member', split_axis=1, concat_axis=0, tiled=T...]
    all_to_all x0 -> x2, waiting for transfers between devices: none -> 9.89 us  [per_device(): lax.all_to_all(latent_out, 'member', split_axis=1, concat_axis=0, tiled=T...]
    all_to_all x1, blocking collectives: 37.5 us -> 47 us  [per_device(): lax.all_to_all(outgoing.reshape(experts, capacity, columns), ('group', 'm...]
    all_to_all x2, starting transfers between devices: 13.4 us -> 7.64 us  [per_device(): lax.all_to_all(partial_sums.astype(jnp.bfloat16).reshape(members, -1, col...]
    ppermute x0 -> x14, waiting for transfers between devices: none -> 5.57 us  [the longest x8 4.69 us: levels_all_put(): extra = ppermute(extra, 'group', tray)]
  transfers between devices with their start and end apart: 5 -> 19, of which waited for: 4 -> 11; matrix products, arithmetic and copies ran while one was open for 9% -> 9% of each run, Pallas kernels for 0% -> 0%
where the time goes in v1:
time: 228 us; the launch traced here: 227 us
  waiting for transfers between devices  54.7 us (24%)
  blocking collectives  47 us (21%)
  starting transfers between devices  44.4 us (19%)
  local copies, waits for them, and re-layouts  36.9 us (16%)
  matrix products  30 us (13%)
  other arithmetic  13.5 us (6%)
    all_to_all x1, blocking collectives, per_device(): lax.all_to_all(outgoing.reshape(experts, capacity, columns), ('group', 'm...  47 us
    all_to_all x1, waiting for transfers between devices, per_device(): lax.all_to_all(arranged, ('group', 'member'), split_axis=0, concat_axis=0...  28.5 us
    ppermute x8, starting transfers between devices, levels_all_put(): extra = ppermute(extra, 'group', tray)  14.4 us
    all_to_all x2, starting transfers between devices, per_device(): lax.all_to_all(latent_out, 'member', split_axis=1, concat_axis=0, tiled=T...  12 us
    all_to_all x2, waiting for transfers between devices, per_device(): lax.all_to_all(partial_sums.astype(jnp.bfloat16).reshape(members, -1, col...  10.8 us
    dot_general x1, matrix products, per_device(): jnp.dot(inner, w_down[0], preferred_element_type=jnp.float32)  10.8 us
    all_to_all x2, waiting for transfers between devices, per_device(): lax.all_to_all(latent_out, 'member', split_axis=1, concat_axis=0, tiled=T...  9.89 us
    all_to_all x2, starting transfers between devices, per_device(): lax.all_to_all(partial_sums.astype(jnp.bfloat16).reshape(members, -1, col...  7.64 us
  transfers between devices with their start and end apart: 19, of which 11 were waited for; matrix products, arithmetic and copies ran while one was open for 9% of the time, Pallas kernels for 0%

profile of v1, /device:TPU:1, one launch (start us, length us, event | category | flops | bytes accessed | tf_op | source)
XLA Modules:
  0.0 227.1 jit_solution(10429592168810431629)
XLA Ops:
  0.0 0.8 compare_and_fusion
  0.8 0.9 copy-done
  1.7 2.3 gather_fusion
  3.9 4.4 %copy.88 = bf16[16,128,576]{2,1,0:T(8,128)(2,1)} copy(bf16[16,128,576]{1,2,0:T(8,128)(2,1)} %gather_fusion) | data formatting | bytes 4718592 | tf_op jit(solution)/shard_map/jit(_take)/gather | solution.py:70
  8.4 2.2 broadcast_select_fusion
  10.6 0.7 fusion.26
  11.2 0.8 copy-done.2
  12.1 0.2 fusion.62
  12.3 2.3 %convolution_convert_fusion.4 = bf16[8,64,512]{2,1,0:T(8,128)(2,1)S(1)} fusion(bf16[16,1,576]{2,1,0:T(2,128)(2,1)S(1)} %copy.89, bf16[16,128,576]{2,1,0:T(8,128)(2,1)} %copy-done.2, f32[8,64]{1,0:T(8,128)S(1)} %fusion.62, f32[8,64,129]{2,1,0:T(8,128)S(1)} %fusion.26), kind=kOutput, calls=%fused_computation.28 | convolution fusion | flops 70207616 | bytes 3168256 | tf_op jit(solution)/shard_map/rhc,rcl->rhl/dot_general | solution.py:80
  14.6 1.1 copy.90
  15.7 8.4 %all-to-all-start = ((bf16[8,64,512]{2,0,1:T(8,128)(2,1)}), bf16[8,64,512]{2,0,1:T(8,128)(2,1)S(1)}, u32[]{:S(2)}, u32[]{:S(2)}) async-start(bf16[8,64,512]{2,0,1:T(8,128)(2,1)} %copy.90), calls=%async_computation | async-start | bytes 1048576 | tf_op jit(solution)/shard_map/all_to_all | solution.py:83
  24.1 2.2 fusion.28
  26.3 0.2 fusion.61
  26.6 2.3 %convolution_convert_fusion.3 = bf16[8,64,512]{2,1,0:T(8,128)(2,1)S(1)} fusion(bf16[16,1,576]{2,1,0:T(2,128)(2,1)S(1)} %copy.89, bf16[16,128,576]{2,1,0:T(8,128)(2,1)} %copy-done.2, f32[8,64]{1,0:T(8,128)S(1)} %fusion.61, f32[8,64,129]{2,1,0:T(8,128)S(1)} %fusion.28), kind=kOutput, calls=%fused_computation.27 | convolution fusion | flops 70207616 | bytes 3168256 | tf_op jit(solution)/shard_map/rhc,rcl->rhl/dot_general | solution.py:80
  28.9 1.1 copy.94
  30.0 4.5 %all-to-all-done = bf16[8,64,512]{2,0,1:T(8,128)(2,1)S(1)} async-done(((bf16[8,64,512]{2,0,1:T(8,128)(2,1)}), bf16[8,64,512]{2,0,1:T(8,128)(2,1)S(1)}, u32[]{:S(2)}, u32[]{:S(2)}) %all-to-all-start) | async-done | bytes 524320 | tf_op jit(solution)/shard_map/all_to_all | solution.py:83
  34.5 3.6 %all-to-all-start.2 = ((bf16[8,64,512]{2,0,1:T(8,128)(2,1)}), bf16[8,64,512]{2,0,1:T(8,128)(2,1)S(1)}, u32[]{:S(2)}, u32[]{:S(2)}) async-start(bf16[8,64,512]{2,0,1:T(8,128)(2,1)} %copy.94), calls=%async_computation.2 | async-start | bytes 1048576 | tf_op jit(solution)/shard_map/all_to_all | solution.py:83
  38.2 0.3 convolution_convert_fusion.6
  38.6 3.3 %collective-permute-start = (bf16[128,512]{0,1:T(8,128)(2,1)S(1)}, bf16[128,512]{0,1:T(8,128)(2,1)S(1)}, u32[]{:S(2)}, u32[]{:S(2)}) collective-permute-start(bf16[128,512]{0,1:T(8,128)(2,1)S(1)} %bitcast.94), channel_id=1, source_target_pairs={{0,16},{16,32},{32,48},{48,64},{64,80},{80,96},{96,112},{112,0},{1... | collective-permute-start | bytes 393224 | tf_op jit(solution)/shard_map/ppermute | solution.py:29
  41.8 5.4 %all-to-all-done.2 = bf16[8,64,512]{2,0,1:T(8,128)(2,1)S(1)} async-done(((bf16[8,64,512]{2,0,1:T(8,128)(2,1)}), bf16[8,64,512]{2,0,1:T(8,128)(2,1)S(1)}, u32[]{:S(2)}, u32[]{:S(2)}) %all-to-all-start.2) | async-done | bytes 524320 | tf_op jit(solution)/shard_map/all_to_all | solution.py:83
  47.2 0.3 convolution_convert_fusion.5
  47.6 4.5 %collective-permute-start.7 = (bf16[128,512]{0,1:T(8,128)(2,1)S(1)}, bf16[128,512]{0,1:T(8,128)(2,1)S(1)}, u32[]{:S(2)}, u32[]{:S(2)}) collective-permute-start(bf16[128,512]{0,1:T(8,128)(2,1)S(1)} %bitcast.91), channel_id=1, source_target_pairs={{0,16},{16,32},{32,48},{48,64},{64,80},{80,96},{96,112},{112,0},{1... | collective-permute-start | bytes 393224 | tf_op jit(solution)/shard_map/ppermute | solution.py:29
  52.4 1.8 collective-permute-start.2
  54.2 2.2 collective-permute-start.9
  56.5 0.7 collective-permute-start.10
  57.4 1.2 collective-permute-start.4
  58.5 0.3 collective-permute-done.3
  58.8 1.5 collective-permute-start.5
  60.4 0.4 collective-permute-start.11
  60.9 0.3 collective-permute-done.10
  61.2 2.2 collective-permute-start.12
  63.5 0.6 collective-permute-done.11
  64.1 1.1 collective-permute-start.13
  65.3 0.3 collective-permute-done.12
  65.6 1.7 collective-permute-done.6
  67.3 2.4 %collective-permute-done.13 = bf16[128,512]{0,1:T(8,128)(2,1)S(1)} collective-permute-done((bf16[128,512]{0,1:T(8,128)(2,1)S(1)}, bf16[128,512]{0,1:T(8,128)(2,1)S(1)}, u32[]{:S(2)}, u32[]{:S(2)}) %collective-permute-start.13) | collective-permute-done | bytes 131104 | tf_op jit(solution)/shard_map/ppermute | solution.py:29
  69.8 0.6 convolution_convert_fusion.1
  70.5 1.3 copy.97
  71.8 3.8 %all-to-all-start.3 = ((bf16[16,64,448]{2,1,0:T(8,128)(2,1)}), bf16[16,64,448]{2,1,0:T(8,128)(2,1)S(1)}, u32[]{:S(2)}, u32[]{:S(2)}) async-start(bf16[16,64,448]{2,1,0:T(8,128)(2,1)} %bitcast.17), calls=%async_computation.3 | async-start | bytes 2097152 | tf_op jit(solution)/shard_map/all_to_all | solution.py:91
  75.9 0.2 fusion.46
  76.2 1.6 convolution_convert_fusion.2
  77.8 2.3 %copy.93 = bf16[1024,448]{1,0:T(8,128)(2,1)} copy(bf16[1024,448]{0,1:T(8,128)(2,1)} %convolution_convert_fusion.2) | data formatting | bytes 1835008 | tf_op jit(solution)/shard_map/convert_element_type | solution.py:92
  80.1 7.6 %all-to-all-done.3 = bf16[16,64,448]{2,1,0:T(8,128)(2,1)S(1)} async-done(((bf16[16,64,448]{2,1,0:T(8,128)(2,1)}), bf16[16,64,448]{2,1,0:T(8,128)(2,1)S(1)}, u32[]{:S(2)}, u32[]{:S(2)}) %all-to-all-start.3) | async-done | bytes 917536 | tf_op jit(solution)/shard_map/all_to_all | solution.py:91
  87.7 3.9 %all-to-all-start.1 = ((bf16[16,64,448]{2,1,0:T(8,128)(2,1)}), bf16[16,64,448]{2,1,0:T(8,128)(2,1)S(1)}, u32[]{:S(2)}, u32[]{:S(2)}) async-start(bf16[16,64,448]{2,1,0:T(8,128)(2,1)} %bitcast.8), calls=%async_computation.1 | async-start | bytes 2097152 | tf_op jit(solution)/shard_map/all_to_all | solution.py:91
  91.9 0.4 fusion.40
  92.4 7.4 %fusion.2 = pred[2048,128]{1,0:T(8,128)(4,1)S(1)} fusion(s32[128,8]{0,1:T(8,128)S(1)} %get-tuple-element.6), kind=kLoop, calls=%fused_computation.5 | loop fusion | flops 3932160 | bytes 266240 | tf_op jit(solution)/shard_map/reduce_or | solution.py:112
  99.9 0.2 convert_reduce_fusion
  100.0 3.2 %all-to-all-done.1 = bf16[16,64,448]{2,1,0:T(8,128)(2,1)S(1)} async-done(((bf16[16,64,448]{2,1,0:T(8,128)(2,1)}), bf16[16,64,448]{2,1,0:T(8,128)(2,1)S(1)}, u32[]{:S(2)}, u32[]{:S(2)}) %all-to-all-start.1) | async-done | bytes 917536 | tf_op jit(solution)/shard_map/all_to_all | solution.py:91
  103.2 0.2 convert_reduce_fusion.1
  103.5 2.0 convolution_convert_fusion
  105.5 2.8 %copy.105 = bf16[2048,448]{1,0:T(8,128)(2,1)S(1)} copy(bf16[2048,448]{0,1:T(8,128)(2,1)} %convolution_convert_fusion) | data formatting | bytes 3670016 | tf_op jit(solution)/shard_map/convert_element_type | solution.py:113
  108.3 47.0 %all_to_all.56 = bf16[128,16,448]{2,1,0:T(8,128)(2,1)S(1)} all-to-all(bf16[128,16,448]{2,1,0:T(8,128)(2,1)S(1)} %bitcast.86), channel_id=1, replica_groups=mesh['group'=8,'member'=16] {'group','member'}, dimensions={0} | all-to-all | bytes 3670016 | tf_op jit(solution)/shard_map/all_to_all | solution.py:114
  155.2 1.4 copy.121
  156.6 3.3 %reshape.88 = bf16[256,3584]{1,0:T(8,128)(2,1)} reshape(bf16[16,16,8,448]{3,2,1,0:T(8,128)(2,1)S(1)} %bitcast.88) | data formatting | bytes 3670016 | tf_op jit(solution)/shard_map/reshape | solution.py:124
  159.9 6.8 %fusion.7 = f32[256,1024]{1,0:T(8,128)} fusion(bf16[256,3584]{1,0:T(8,128)(2,1)} %reshape.88, bf16[1,3584,1024]{2,1,0:T(8,128)(2,1)} %param.21), kind=kOutput, calls=%fused_computation.10 | convolution fusion | flops 1879048192 | bytes 10223616 | tf_op jit(solution)/shard_map/dot_general | solution.py:126
  166.8 10.8 %fusion.9 = bf16[256,3584]{1,0:T(8,128)(2,1)} fusion(bf16[1,1024,3584]{2,1,0:T(8,128)(2,1)} %param.23, bf16[256,3584]{1,0:T(8,128)(2,1)S(1)} %copy-done.4, bf16[1,3584,1024]{2,1,0:T(8,128)(2,1)} %param.22, f32[256,1024]{1,0:T(8,128)} %fusion.7), kind=kOutput, calls=%fused_computation.12 | convolution fusion | flops 3760586752 | bytes 19398656 | tf_op jit(solution)/shard_map/dot_general | solution.py:129
  177.6 3.9 %reshape.89 = bf16[16,16,8,448]{3,2,1,0:T(8,128)(2,1)S(1)} reshape(bf16[256,3584]{1,0:T(8,128)(2,1)} %fusion.9) | data formatting | bytes 3670016 | tf_op jit(solution)/shard_map/reshape | solution.py:131
  181.5 2.0 copy.107
  183.5 5.9 %all-to-all-start.5 = ((bf16[128,16,448]{2,1,0:T(8,128)(2,1)}), bf16[128,16,448]{2,1,0:T(8,128)(2,1)}, u32[]{:S(2)}, u32[]{:S(2)}) async-start(bf16[128,16,448]{2,1,0:T(8,128)(2,1)} %bitcast.30), calls=%async_computation.5 | async-start | bytes 4194304 | tf_op jit(solution)/shard_map/all_to_all | solution.py:135
  189.5 0.7 copy.99
  190.3 28.5 %all-to-all-done.5 = bf16[128,16,448]{2,1,0:T(8,128)(2,1)} async-done(((bf16[128,16,448]{2,1,0:T(8,128)(2,1)}), bf16[128,16,448]{2,1,0:T(8,128)(2,1)}, u32[]{:S(2)}, u32[]{:S(2)}) %all-to-all-start.5) | async-done | bytes 1835040 | tf_op jit(solution)/shard_map/all_to_all | solution.py:135
  218.8 6.0 %gather_fusion.1 = bf16[1024,448]{1,0:T(8,128)(2,1)S(1)} fusion(bf16[2048,448]{1,0:T(8,128)(2,1)} %bitcast.31, s32[1024]{0:T(1024)S(1)} %broadcast_clamp_fusion), kind=kCustom, calls=%fused_computation.1 | custom fusion | bytes 1839104 | tf_op jit(solution)/shard_map/gather | solution.py:139
  224.8 1.6 fusion.12
  226.4 0.8 copy.109
  (73 shorter events, 2.2 us)
Async XLA Ops:
  0.0 1.7 copy-start
  3.9 4.4 %copy-start.6 = (bf16[16,576]{1,0:T(8,128)(2,1)S(1)}, bf16[16,576]{1,0:T(8,128)(2,1)}, u32[]{:S(2)}) copy-start(bf16[16,576]{1,0:T(8,128)(2,1)} %param.14) | copy-start | bytes 55300
  8.3 2.2 copy-start.9
  10.5 1.5 copy-start.2
  15.7 18.8 %all-to-all-start = ((bf16[8,64,512]{2,0,1:T(8,128)(2,1)}), bf16[8,64,512]{2,0,1:T(8,128)(2,1)S(1)}, u32[]{:S(2)}, u32[]{:S(2)}) async-start(bf16[8,64,512]{2,0,1:T(8,128)(2,1)} %copy.90), calls=%async_computation | async-start | bytes 1048576 | tf_op jit(solution)/shard_map/all_to_all | solution.py:83
  26.5 11.7 %copy-start.3 = (bf16[4,512,128]{2,1,0:T(8,128)(2,1)S(1)}, bf16[4,512,128]{2,1,0:T(8,128)(2,1)}, u32[]{:S(2)}) copy-start(bf16[4,512,128]{2,1,0:T(8,128)(2,1)} %param.16) | copy-start | bytes 1572868
  34.5 12.7 %all-to-all-start.2 = ((bf16[8,64,512]{2,0,1:T(8,128)(2,1)}), bf16[8,64,512]{2,0,1:T(8,128)(2,1)S(1)}, u32[]{:S(2)}, u32[]{:S(2)}) async-start(bf16[8,64,512]{2,0,1:T(8,128)(2,1)} %copy.94), calls=%async_computation.2 | async-start | bytes 1048576 | tf_op jit(solution)/shard_map/all_to_all | solution.py:83
  38.6 13.8 %collective-permute-start = (bf16[128,512]{0,1:T(8,128)(2,1)S(1)}, bf16[128,512]{0,1:T(8,128)(2,1)S(1)}, u32[]{:S(2)}, u32[]{:S(2)}) collective-permute-start(bf16[128,512]{0,1:T(8,128)(2,1)S(1)} %bitcast.94), channel_id=1, source_target_pairs={{0,16},{16,32},{32,48},{48,64},{64,80},{80,96},{96,112},{112,0},{1... | collective-permute-start | bytes 393224 | tf_op jit(solution)/shard_map/ppermute | solution.py:29
  41.8 12.3 %collective-permute-start.1 = (bf16[128,512]{0,1:T(8,128)(2,1)S(1)}, bf16[128,512]{0,1:T(8,128)(2,1)S(1)}, u32[]{:S(2)}, u32[]{:S(2)}) collective-permute-start(bf16[128,512]{0,1:T(8,128)(2,1)S(1)} %bitcast.95), channel_id=1, source_target_pairs={{0,112},{16,0},{32,16},{48,32},{64,48},{80,64},{96,80},{112,96},{1... | collective-permute-start | bytes 393224 | tf_op jit(solution)/shard_map/ppermute | solution.py:39
  47.6 6.7 %collective-permute-start.7 = (bf16[128,512]{0,1:T(8,128)(2,1)S(1)}, bf16[128,512]{0,1:T(8,128)(2,1)S(1)}, u32[]{:S(2)}, u32[]{:S(2)}) collective-permute-start(bf16[128,512]{0,1:T(8,128)(2,1)S(1)} %bitcast.91), channel_id=1, source_target_pairs={{0,16},{16,32},{32,48},{48,64},{64,80},{80,96},{96,112},{112,0},{1... | collective-permute-start | bytes 393224 | tf_op jit(solution)/shard_map/ppermute | solution.py:29
  52.0 4.5 %collective-permute-start.8 = (bf16[128,512]{0,1:T(8,128)(2,1)S(1)}, bf16[128,512]{0,1:T(8,128)(2,1)S(1)}, u32[]{:S(2)}, u32[]{:S(2)}) collective-permute-start(bf16[128,512]{0,1:T(8,128)(2,1)S(1)} %bitcast.92), channel_id=1, source_target_pairs={{0,112},{16,0},{32,16},{48,32},{64,48},{80,64},{96,80},{112,96},{1... | collective-permute-start | bytes 393224 | tf_op jit(solution)/shard_map/ppermute | solution.py:39
  52.2 17.6 %copy-start.10 = (bf16[512,448]{0,1:T(8,128)(2,1)S(1)}, bf16[512,448]{0,1:T(8,128)(2,1)}, u32[]{:S(2)}) copy-start(bf16[512,448]{0,1:T(8,128)(2,1)} %param.17) | copy-start | bytes 1376260
  52.4 5.0 %collective-permute-start.2 = (bf16[128,512]{0,1:T(8,128)(2,1)S(1)}, bf16[128,512]{0,1:T(8,128)(2,1)S(1)}, u32[]{:S(2)}, u32[]{:S(2)}) collective-permute-start(bf16[128,512]{0,1:T(8,128)(2,1)S(1)} %collective-permute-done), channel_id=1, source_target_pairs={{0,16},{16,32},{32,48},{48,64},{64,80},{80,96},{96,112},{112,0},{1... | collective-permute-start | bytes 393224 | tf_op jit(solution)/shard_map/ppermute | solution.py:29
  54.1 4.7 %collective-permute-start.3 = (bf16[128,512]{0,1:T(8,128)(2,1)S(1)}, bf16[128,512]{0,1:T(8,128)(2,1)S(1)}, u32[]{:S(2)}, u32[]{:S(2)}) collective-permute-start(bf16[128,512]{0,1:T(8,128)(2,1)S(1)} %collective-permute-done.1), channel_id=1, source_target_pairs={{0,112},{16,0},{32,16},{48,32},{64,48},{80,64},{96,80},{112,96},{1... | collective-permute-start | bytes 393224 | tf_op jit(solution)/shard_map/ppermute | solution.py:39
  54.2 6.2 %collective-permute-start.9 = (bf16[128,512]{0,1:T(8,128)(2,1)S(1)}, bf16[128,512]{0,1:T(8,128)(2,1)S(1)}, u32[]{:S(2)}, u32[]{:S(2)}) collective-permute-start(bf16[128,512]{0,1:T(8,128)(2,1)S(1)} %collective-permute-done.7), channel_id=1, source_target_pairs={{0,16},{16,32},{32,48},{48,64},{64,80},{80,96},{96,112},{112,0},{1... | collective-permute-start | bytes 393224 | tf_op jit(solution)/shard_map/ppermute | solution.py:29
  56.5 4.7 %collective-permute-start.10 = (bf16[128,512]{0,1:T(8,128)(2,1)S(1)}, bf16[128,512]{0,1:T(8,128)(2,1)S(1)}, u32[]{:S(2)}, u32[]{:S(2)}) collective-permute-start(bf16[128,512]{0,1:T(8,128)(2,1)S(1)} %collective-permute-done.8), channel_id=1, source_target_pairs={{0,112},{16,0},{32,16},{48,32},{64,48},{80,64},{96,80},{112,96},{1... | collective-permute-start | bytes 393224 | tf_op jit(solution)/shard_map/ppermute | solution.py:39
  57.4 6.1 %collective-permute-start.4 = (bf16[128,512]{0,1:T(8,128)(2,1)S(1)}, bf16[128,512]{0,1:T(8,128)(2,1)S(1)}, u32[]{:S(2)}, u32[]{:S(2)}) collective-permute-start(bf16[128,512]{0,1:T(8,128)(2,1)S(1)} %collective-permute-done.2), channel_id=1, source_target_pairs={{0,16},{16,32},{32,48},{48,64},{64,80},{80,96},{96,112},{112,0},{1... | collective-permute-start | bytes 393224 | tf_op jit(solution)/shard_map/ppermute | solution.py:29
  58.8 6.5 %collective-permute-start.5 = (bf16[128,512]{0,1:T(8,128)(2,1)S(1)}, bf16[128,512]{0,1:T(8,128)(2,1)S(1)}, u32[]{:S(2)}, u32[]{:S(2)}) collective-permute-start(bf16[128,512]{0,1:T(8,128)(2,1)S(1)} %collective-permute-done.3), channel_id=1, source_target_pairs={{0,112},{16,0},{32,16},{48,32},{64,48},{80,64},{96,80},{112,96},{1... | collective-permute-start | bytes 393224 | tf_op jit(solution)/shard_map/ppermute | solution.py:39
  60.4 3.8 %collective-permute-start.11 = (bf16[128,512]{0,1:T(8,128)(2,1)S(1)}, bf16[128,512]{0,1:T(8,128)(2,1)S(1)}, u32[]{:S(2)}, u32[]{:S(2)}) collective-permute-start(bf16[128,512]{0,1:T(8,128)(2,1)S(1)} %collective-permute-done.9), channel_id=1, source_target_pairs={{0,16},{16,32},{32,48},{48,64},{64,80},{80,96},{96,112},{112,0},{1... | collective-permute-start | bytes 393224 | tf_op jit(solution)/shard_map/ppermute | solution.py:29
  61.2 4.4 %collective-permute-start.12 = (bf16[128,512]{0,1:T(8,128)(2,1)S(1)}, bf16[128,512]{0,1:T(8,128)(2,1)S(1)}, u32[]{:S(2)}, u32[]{:S(2)}) collective-permute-start(bf16[128,512]{0,1:T(8,128)(2,1)S(1)} %collective-permute-done.10), channel_id=1, source_target_pairs={{0,112},{16,0},{32,16},{48,32},{64,48},{80,64},{96,80},{112,96},{1... | collective-permute-start | bytes 393224 | tf_op jit(solution)/shard_map/ppermute | solution.py:39
  63.5 3.8 %collective-permute-start.6 = (bf16[128,512]{0,1:T(8,128)(2,1)S(1)}, bf16[128,512]{0,1:T(8,128)(2,1)S(1)}, u32[]{:S(2)}, u32[]{:S(2)}) collective-permute-start(bf16[128,512]{0,1:T(8,128)(2,1)S(1)} %collective-permute-done.4), channel_id=1, source_target_pairs={{0,16},{16,32},{32,48},{48,64},{64,80},{80,96},{96,112},{112,0},{1... | collective-permute-start | bytes 393224 | tf_op jit(solution)/shard_map/ppermute | solution.py:29
  64.1 5.6 %collective-permute-start.13 = (bf16[128,512]{0,1:T(8,128)(2,1)S(1)}, bf16[128,512]{0,1:T(8,128)(2,1)S(1)}, u32[]{:S(2)}, u32[]{:S(2)}) collective-permute-start(bf16[128,512]{0,1:T(8,128)(2,1)S(1)} %collective-permute-done.11), channel_id=1, source_target_pairs={{0,16},{16,32},{32,48},{48,64},{64,80},{80,96},{96,112},{112,0},{1... | collective-permute-start | bytes 393224 | tf_op jit(solution)/shard_map/ppermute | solution.py:29
  70.5 5.1 %copy-start.7 = (s32[128,8]{0,1:T(8,128)S(1)}, s32[128,8]{0,1:T(8,128)}, u32[]{:S(2)}) copy-start(s32[128,8]{0,1:T(8,128)} %param.19) | copy-start | bytes 12292
  71.8 4.4 %copy-start.11 = (bf16[512,448]{0,1:T(8,128)(2,1)S(1)}, bf16[512,448]{0,1:T(8,128)(2,1)}, u32[]{:S(2)}) copy-start(bf16[512,448]{0,1:T(8,128)(2,1)} %param.17) | copy-start | bytes 1376260
  71.8 15.8 %all-to-all-start.3 = ((bf16[16,64,448]{2,1,0:T(8,128)(2,1)}), bf16[16,64,448]{2,1,0:T(8,128)(2,1)S(1)}, u32[]{:S(2)}, u32[]{:S(2)}) async-start(bf16[16,64,448]{2,1,0:T(8,128)(2,1)} %bitcast.17), calls=%async_computation.3 | async-start | bytes 2097152 | tf_op jit(solution)/shard_map/all_to_all | solution.py:91
  77.8 13.9 %copy-start.5 = (bf16[128,448]{0,1:T(8,128)(2,1)S(1)}, bf16[128,448]{0,1:T(8,128)(2,1)}, u32[]{:S(2)}) copy-start(bf16[128,448]{0,1:T(8,128)(2,1)} %param.18) | copy-start | bytes 344068
  87.7 15.6 %all-to-all-start.1 = ((bf16[16,64,448]{2,1,0:T(8,128)(2,1)}), bf16[16,64,448]{2,1,0:T(8,128)(2,1)S(1)}, u32[]{:S(2)}, u32[]{:S(2)}) async-start(bf16[16,64,448]{2,1,0:T(8,128)(2,1)} %bitcast.8), calls=%async_computation.1 | async-start | bytes 2097152 | tf_op jit(solution)/shard_map/all_to_all | solution.py:91
  159.9 6.8 %copy-start.4 = (bf16[256,3584]{1,0:T(8,128)(2,1)S(1)}, bf16[256,3584]{1,0:T(8,128)(2,1)}, u32[]{:S(2)}) copy-start(bf16[256,3584]{1,0:T(8,128)(2,1)} %reshape.88) | copy-start | bytes 5505028
  183.5 6.1 %copy-start.8 = (f32[128,8]{0,1:T(8,128)S(1)}, f32[128,8]{0,1:T(8,128)}, u32[]{:S(2)}) copy-start(f32[128,8]{0,1:T(8,128)} %param.20) | copy-start | bytes 12292
  183.5 35.3 %all-to-all-start.5 = ((bf16[128,16,448]{2,1,0:T(8,128)(2,1)}), bf16[128,16,448]{2,1,0:T(8,128)(2,1)}, u32[]{:S(2)}, u32[]{:S(2)}) async-start(bf16[128,16,448]{2,1,0:T(8,128)(2,1)} %bitcast.30), calls=%async_computation.5 | async-start | bytes 4194304 | tf_op jit(solution)/shard_map/all_to_all | solution.py:135
  218.8 8.4 %copy-start.1 = (bf16[16,128,576]{1,2,0:T(8,128)(2,1)S(1)}, bf16[16,128,576]{1,2,0:T(8,128)(2,1)}, u32[]{:S(2)}) copy-start(bf16[16,128,576]{1,2,0:T(8,128)(2,1)} %param.13) | copy-start | bytes 7077892
